TPU v7x, 32 devices: a whole 2x2x4 slice. The times are simulated.
32 devices in a mesh: layer: 2 (over x), row: 4 (over y, core), col: 4 (over z).
Axes of the slice: x: 2, y: 2, z: 4, core: 2. Of those that a mesh axis runs over, the one named last changes fastest.
Arguments:
- left_matrix: bfloat16 [8192, 1024], P('row', ('layer', 'col')), may hold values from -6 to 6
- square_term: bfloat16 [1024, 1024], P(('layer', 'row'), 'col'), may hold values from -0.5 to 0.5
- block_pattern: int32 [64, 8], replicated, may hold values from 0 to 1, as said below
- keep_mask: int32 [64, 8], replicated, may hold values 0 or 1
Outputs:
- product: bfloat16 [8192, 1024], P('row', 'col')
Inputs may be any that keep to these rules, and one draw needn't show every extreme that they name: `block_pattern`: in each aligned group of 16 block rows, every block column holds 1 to 8 stored blocks; some group holds exactly 8.
All inputs are finite; a program needn't handle non-finite values.
Results may differ from a plain program's by a relative error of at most 0.0038.
Values may be sent and summed in bfloat16 or wider, within the bound.
No kernel may reach another device: no remote copies, remote signals or barrier semaphores. Data moves between devices by JAX's collectives and lax.ppermute only.
A program may use at most 64 MiB of HBM per device.

v0:
```python
import jax
import jax.numpy as jnp
from jax import lax
from jax.sharding import PartitionSpec as P

BLK = 128
GROUP = 16
CAP = 8


def slot_table(pattern):
    stored = (pattern > 0).astype(jnp.int32)
    rows = pattern.shape[0]
    groups = rows // GROUP
    grouped = stored.reshape(groups, GROUP, -1)
    slot = jnp.cumsum(grouped, axis=1) - 1
    group_base = (jnp.arange(groups, dtype=jnp.int32) * CAP)[:, None, None]
    slot = (slot + group_base).reshape(rows, -1)
    return (stored, slot)


def per_device(left_matrix, square_term, block_pattern, keep_mask):
    row_idx = lax.axis_index("row")
    col_idx = lax.axis_index("col")
    layer_idx = lax.axis_index("layer")
    row_count = lax.axis_size("row")
    col_count = lax.axis_size("col")
    rows_local = left_matrix.shape[0]
    row_blocks = rows_local // BLK
    inner_blocks = left_matrix.shape[1] // BLK
    inner_local = square_term.shape[0]
    cols_local = square_term.shape[1]
    col_blocks = cols_local // BLK
    slots = row_blocks // GROUP * CAP
    total_inner_blocks = block_pattern.shape[1]
    inner_start = (layer_idx * col_count + col_idx) * inner_blocks
    pattern_patch = lax.dynamic_slice(
        block_pattern, (row_idx * row_blocks, inner_start), (row_blocks, inner_blocks)
    )
    stored, slot = slot_table(pattern_patch)
    slot_ids = jnp.arange(slots, dtype=jnp.int32)
    hit = (stored[:, :, None] > 0) & (slot[:, :, None] == slot_ids[None, None, :])
    source_row = jnp.sum(
        jnp.where(hit, jnp.arange(row_blocks, dtype=jnp.int32)[:, None, None], 0), axis=0
    )
    blocks = left_matrix.reshape(row_blocks, BLK, inner_blocks, BLK).transpose(2, 0, 1, 3)
    flat_blocks = blocks.reshape(inner_blocks * row_blocks, BLK, BLK)
    take_idx = source_row + (jnp.arange(inner_blocks, dtype=jnp.int32) * row_blocks)[:, None]
    packed = jnp.take(flat_blocks, take_idx.reshape(-1), axis=0)
    packed = packed.reshape(inner_blocks, slots, BLK, BLK)
    gathered = lax.all_gather(packed, ("layer", "col"), axis=0, tiled=True)
    first_inner = (layer_idx * row_count + row_idx) * inner_local
    first_col = col_idx * cols_local
    inner_pos = first_inner + lax.broadcasted_iota(jnp.int32, (inner_local, cols_local), 0)
    col_pos = first_col + lax.broadcasted_iota(jnp.int32, (inner_local, cols_local), 1)
    unit = jnp.where(inner_pos == col_pos, jnp.float32(1.5), jnp.float32(0.0))
    right_factor = (unit - 0.5 * square_term.astype(jnp.float32)).astype(jnp.bfloat16)
    right_full = lax.all_gather(right_factor, ("layer", "row"), axis=0, tiled=True)
    panel_pattern = lax.dynamic_slice(
        block_pattern, (row_idx * row_blocks, 0), (row_blocks, total_inner_blocks)
    )
    p_stored, p_slot = slot_table(panel_pattern)
    gather_idx = jnp.arange(total_inner_blocks, dtype=jnp.int32)[None, :] * slots + jnp.clip(
        p_slot, 0, slots - 1
    )
    flat_packed = gathered.reshape(total_inner_blocks * slots, BLK, BLK)
    right_blocks = right_full.reshape(total_inner_blocks, BLK, cols_local)

    def chunk_sum(first, count):
        idx = lax.dynamic_slice_in_dim(gather_idx, first, count, axis=1)
        keep = lax.dynamic_slice_in_dim(p_stored, first, count, axis=1)
        dense = jnp.take(flat_packed, idx.reshape(-1), axis=0)
        dense = dense.reshape(row_blocks, count, BLK, BLK)
        dense = jnp.where(keep[:, :, None, None] > 0, dense, jnp.zeros_like(dense))
        rhs = lax.dynamic_slice_in_dim(right_blocks, first, count, axis=0)
        return jnp.einsum("ijab,jbc->iac", dense, rhs, preferred_element_type=jnp.float32)

    dense_bytes = row_blocks * total_inner_blocks * BLK * BLK * 2
    chunks = max(1, dense_bytes // (4 << 20))
    while total_inner_blocks % chunks:
        chunks += 1
    if chunks == 1:
        full_sum = chunk_sum(0, total_inner_blocks)
    else:
        per_chunk = total_inner_blocks // chunks

        def body(c, acc):
            return acc + chunk_sum(c * per_chunk, per_chunk)

        full_sum = lax.fori_loop(
            0, chunks, body, jnp.zeros((row_blocks, BLK, cols_local), jnp.float32)
        )
    full_sum = full_sum.reshape(rows_local, cols_local)
    keep_patch = lax.dynamic_slice(
        keep_mask, (row_idx * row_blocks, col_idx * col_blocks), (row_blocks, col_blocks)
    )
    keep_full = jnp.repeat(jnp.repeat(keep_patch, BLK, axis=0), BLK, axis=1)
    kept = jnp.where(keep_full > 0, full_sum, jnp.zeros_like(full_sum))
    return kept.astype(jnp.bfloat16)


def solution(mesh):
    return jax.shard_map(
        per_device,
        mesh=mesh,
        in_specs=(P("row", ("layer", "col")), P(("layer", "row"), "col"), P(), P()),
        out_specs=P("row", "col"),
        check_vma=False,
    )
```

profile of v0, /device:TPU:0, one launch (start us, length us, event | category | flops | bytes accessed | tf_op | source)
XLA Modules:
  0.0 81.9 jit_solution(10551937533751118428)
XLA Ops:
  6.5 0.0 copy-start
  6.5 0.0 all-gather.2.cloned.1.call-start
  6.5 0.8 %compare_bitcast_fusion = (pred[16]{0:T(512)(128)(4,1)S(1)}, s32[16,1]{0,1:T(1,128)S(1)}) fusion(s32[64,8]{0,1:T(8,128)} %param.6, s32[]{:T(128)S(6)} %select_n.84, s32[]{:T(128)S(6)} %select_n.87), kind=kLoop, calls=%fused_computation.29 | loop fusion | flops 48 | bytes 152 | tf_op jit(solution)/shard_map/gt | solution.py:42
  7.4 0.1 copy.39
  7.5 0.1 add_reduce_fusion
  7.6 0.1 select_reduce_fusion
  7.8 0.0 copy-done
  7.8 0.6 gather_fusion
  8.4 0.8 bitcast_select_fusion
  9.2 0.0 all-gather.2.cloned.1.call-update
  9.2 0.8 convert_compare_fusion
  10.0 0.1 copy.36
  10.1 0.1 min.15
  10.2 0.1 copy.37
  10.3 0.1 add.128
  10.3 0.1 compare_and_fusion
  10.4 0.1 copy.38
  10.5 0.1 copy.35
  10.6 0.8 dynamic-slice_compare_fusion.1
  11.4 0.1 broadcast_bitcast_fusion
  11.5 0.1 broadcast_in_dim.66
  11.6 0.6 copy.43
  12.3 0.9 %subtract_convert_fusion = bf16[128,256]{1,0:T(8,128)(2,1)S(1)} fusion(bf16[128,256]{1,0:T(8,128)(2,1)} %param.5, s32[256]{0:T(256)S(1)} %iota_add_fusion, s32[128]{0:T(128)S(1)} %iota_add_fusion.1), kind=kLoop, calls=%fused_computation.9 | loop fusion | flops 196608 | bytes 132608 | tf_op jit(solution)/shard_map/convert_element_type | solution.py:57
  13.2 12.6 %all_gather.7 = bf16[1024,256]{1,0:T(8,128)(2,1)S(1)} all-gather(bf16[128,256]{1,0:T(8,128)(2,1)S(1)} %subtract_convert_fusion), channel_id=1, replica_groups=mesh['layer'=2,'row'=4,'col'=4] {'layer','row'}, dimensions={0}, use_global_device_ids=true | all-gather | bytes 589824 | tf_op jit(solution)/shard_map/all_gather | solution.py:58
  25.8 36.2 %all-gather.2.cloned.1.call-done = bf16[8,8,128,128]{3,2,1,0:T(8,128)(2,1)} async-done(((bf16[1,8,128,128]{3,2,1,0:T(8,128)(2,1)}), bf16[8,8,128,128]{3,2,1,0:T(8,128)(2,1)}) %all-gather.2.cloned.1.call-update) | async-done | bytes 2097168 | tf_op jit(solution)/shard_map/all_gather | solution.py:51
  62.0 4.6 %gather_fusion.1 = bf16[128,128,128]{2,1,0:T(8,128)(2,1)} fusion(bf16[64,128,128]{2,1,0:T(8,128)(2,1)} %bitcast.42, s32[1024]{0:T(1024)S(1)} %pad_clamp_fusion), kind=kCustom, calls=%fused_computation.1 | custom fusion | bytes 8389120 | tf_op jit(solution)/shard_map/jit(_take)/gather | solution.py:72
  66.6 2.6 %select_bitcast_fusion = bf16[16,128,128,8]{2,1,3,0:T(8,128)(2,1)S(1)} fusion(bf16[16,8,128,128]{3,2,1,0:T(8,128)(2,1)} %bitcast.41, pred[16,8]{1,0:T(8,128)(4,1)S(1)} %copy.38, pred[16,8]{1,0:T(8,128)(4,1)S(1)} %copy.35), kind=kLoop, calls=%fused_computation.4 | loop fusion | flops 4194304 | bytes 8388864 | tf_op jit(solution)/shard_map/ijab,jbc->iac/dot_general | solution.py:76
  69.2 3.5 %copy.41 = bf16[16,128,128,8]{2,3,1,0:T(8,128)(2,1)S(1)} copy(bf16[16,128,128,8]{2,1,3,0:T(8,128)(2,1)S(1)} %select_bitcast_fusion) | data formatting | bytes 8388608 | tf_op jit(solution)/shard_map/ijab,jbc->iac/dot_general | solution.py:76
  72.7 2.3 %fusion.8 = bf16[2048,256]{1,0:T(8,128)(2,1)} fusion(pred[2048,256]{1,0:T(32,128)(4,1)S(1)} %copy.43, bf16[8,128,256]{2,1,0:T(8,128)(2,1)S(1)} %bitcast.45, bf16[2048,128,8]{1,2,0:T(8,128)(2,1)S(1)} %bitcast.43), kind=kOutput, calls=%fused_computation.7 | convolution fusion | flops 1074790400 | bytes 6291456 | tf_op jit(solution)/shard_map/ijab,jbc->iac/dot_general | solution.py:76
  (14 shorter events, 0.2 us)
Async XLA Ops:
  6.5 1.2 %copy-start = (bf16[2048,128]{1,0:T(8,128)(2,1)S(1)}, bf16[2048,128]{1,0:T(8,128)(2,1)}, u32[]{:S(2)}) copy-start(bf16[2048,128]{1,0:T(8,128)(2,1)} %param.4) | copy-start | bytes 1572868
  6.5 55.5 %all-gather.2.cloned.1.call-start = ((), (), s32[]{:S(2)}) async-start(), calls=%async_computation | async-start | bytes 2359296 | tf_op jit(solution)/shard_map/all_gather | solution.py:51
Sparse Core Ops, SparseCore 0:
  9.5 52.4 all-gather.1
where the time goes:
time: 82.1 us; the launch traced here: 81.9 us
  waiting for transfers between devices  36.2 us (44%)
  between operations  13.5 us (16%)
  blocking collectives  12.6 us (15%)
  local copies, waits for them, and re-layouts  10.2 us (12%)
  other arithmetic  7.08 us (9%)
  matrix products  2.27 us (3%)
    all_gather x1, waiting for transfers between devices, per_device(): gathered = lax.all_gather(packed, ('layer', 'col'), axis=0, tiled=True)  36.2 us
    all_gather x1, blocking collectives, per_device(): lax.all_gather(right_factor, ('layer', 'row'), axis=0, tiled=True)  12.6 us
    gather x1, local copies, waits for them, and re-layouts, chunk_sum(): dense = jnp.take(flat_packed, idx.reshape(-1), axis=0)  4.6 us
    dot_general x1, local copies, waits for them, and re-layouts, chunk_sum(): jnp.einsum('ijab,jbc->iac', dense, rhs, preferred_element_type=jnp.float32)  3.54 us
    dot_general x1, other arithmetic, chunk_sum(): jnp.einsum('ijab,jbc->iac', dense, rhs, preferred_element_type=jnp.float32)  2.56 us
    dot_general x1, matrix products, chunk_sum(): jnp.einsum('ijab,jbc->iac', dense, rhs, preferred_element_type=jnp.float32)  2.27 us
  transfers between devices with their start and end apart: 1, of which 1 were waited for; matrix products, arithmetic and copies ran while one was open for 5% of the time, Pallas kernels for 0%

commit v1 on v0

--- a/solution.py
+++ b/solution.py
@@ -48,7 +48,28 @@
     take_idx = source_row + (jnp.arange(inner_blocks, dtype=jnp.int32) * row_blocks)[:, None]
     packed = jnp.take(flat_blocks, take_idx.reshape(-1), axis=0)
     packed = packed.reshape(inner_blocks, slots, BLK, BLK)
-    gathered = lax.all_gather(packed, ("layer", "col"), axis=0, tiled=True)
+    size, index, rows_2 = (
+        lax.axis_size(("layer", "col")),
+        lax.axis_index(("layer", "col")),
+        packed.shape[0],
+    )
+    right = [(i, (i + 1) % size) for i in range(size)]
+    left = [(i, (i - 1) % size) for i in range(size)]
+    filled = jnp.zeros((*packed.shape[:0], size * rows_2, *packed.shape[0 + 1 :]), packed.dtype)
+    filled = lax.dynamic_update_slice_in_dim(filled, packed, index * rows_2, axis=0)
+    from_left = from_right = packed
+    half = size // 2
+    for step in range(1, half + 1):
+        from_left = lax.ppermute(from_left, ("layer", "col"), right)
+        filled = lax.dynamic_update_slice_in_dim(
+            filled, from_left, (index - step) % size * rows_2, axis=0
+        )
+        if step < size - half:
+            from_right = lax.ppermute(from_right, ("layer", "col"), left)
+            filled = lax.dynamic_update_slice_in_dim(
+                filled, from_right, (index + step) % size * rows_2, axis=0
+            )
+    gathered = filled
     first_inner = (layer_idx * row_count + row_idx) * inner_local
     first_col = col_idx * cols_local
     inner_pos = first_inner + lax.broadcasted_iota(jnp.int32, (inner_local, cols_local), 0)

time: 82.1 us -> 70.5 us (0.86)
  between operations: 13.5 us -> 0.19 us
  waiting for transfers between devices: 36.2 us -> 23.9 us
  starting transfers between devices: 0.01 us -> 10.1 us
  local copies, waits for them, and re-layouts: 10.2 us -> 13 us
  blocking collectives: 12.6 us -> 15.1 us
  other arithmetic: 7.08 us -> 5.65 us
    all_gather x1 -> x0, waiting for transfers between devices: 36.2 us -> none  [per_device(): gathered = lax.all_gather(packed, ('layer', 'col'), axis=0, tiled=True)]
    ppermute x0 -> x7, waiting for transfers between devices: none -> 23.9 us  [the longest x3 17.9 us: per_device(): from_right = lax.ppermute(from_right, ('layer', 'col'), left)]
    ppermute x0 -> x7, starting transfers between devices: none -> 10.1 us  [the longest x4 6.82 us: per_device(): from_left = lax.ppermute(from_left, ('layer', 'col'), right)]
    dynamic_update_slice x0 -> x7, local copies, waits for them, and re-layouts: none -> 3.11 us  [the longest x4 2.05 us: per_device(): lax.dynamic_update_slice_in_dim(filled, from_left, (index - step) % size...]
    all_gather x1, blocking collectives: 12.6 us -> 15.1 us  [per_device(): lax.all_gather(right_factor, ('layer', 'row'), axis=0, tiled=True)]
    gather x1, local copies, waits for them, and re-layouts: 4.6 us -> 3.02 us  [chunk_sum(): dense = jnp.take(flat_packed, idx.reshape(-1), axis=0)]
    dynamic_update_slice x0 -> x1, other arithmetic: none -> 0.9 us  [per_device(): lax.dynamic_update_slice_in_dim(filled, packed, index * rows_2, axis=0)]
    convert_element_type x1, other arithmetic: 0.93 us -> 0.09 us  [per_device(): (unit - 0.5 * square_term.astype(jnp.float32)).astype(jnp.bfloat16)]
  transfers between devices with their start and end apart: 1 -> 7, of which waited for: 1 -> 3; matrix products, arithmetic and copies ran while one was open for 5% -> 9% of each run, Pallas kernels for 0% -> 0%
where the time goes in v1:
time: 70.5 us; the launch traced here: 70.2 us
  waiting for transfers between devices  23.9 us (34%)
  blocking collectives  15.1 us (21%)
  local copies, waits for them, and re-layouts  13 us (18%)
  starting transfers between devices  10.1 us (14%)
  other arithmetic  5.65 us (8%)
  matrix products  2.27 us (3%)
    ppermute x3, waiting for transfers between devices, per_device(): from_right = lax.ppermute(from_right, ('layer', 'col'), left)  17.9 us
    all_gather x1, blocking collectives, per_device(): lax.all_gather(right_factor, ('layer', 'row'), axis=0, tiled=True)  15.1 us
    ppermute x4, starting transfers between devices, per_device(): from_left = lax.ppermute(from_left, ('layer', 'col'), right)  6.82 us
    ppermute x4, waiting for transfers between devices, per_device(): from_left = lax.ppermute(from_left, ('layer', 'col'), right)  6.01 us
    dot_general x1, local copies, waits for them, and re-layouts, chunk_sum(): jnp.einsum('ijab,jbc->iac', dense, rhs, preferred_element_type=jnp.float32)  3.55 us
    ppermute x3, starting transfers between devices, per_device(): from_right = lax.ppermute(from_right, ('layer', 'col'), left)  3.3 us
    gather x1, local copies, waits for them, and re-layouts, chunk_sum(): dense = jnp.take(flat_packed, idx.reshape(-1), axis=0)  3.02 us
    dot_general x1, other arithmetic, chunk_sum(): jnp.einsum('ijab,jbc->iac', dense, rhs, preferred_element_type=jnp.float32)  2.56 us
  transfers between devices with their start and end apart: 7, of which 3 were waited for; matrix products, arithmetic and copies ran while one was open for 9% of the time, Pallas kernels for 0%

profile of v1, /device:TPU:0, one launch (start us, length us, event | category | flops | bytes accessed | tf_op | source)
XLA Modules:
  0.0 70.2 jit_solution(3054694393368315144)
XLA Ops:
  0.0 0.0 copy-start
  0.0 0.8 %compare_bitcast_fusion = (pred[16]{0:T(512)(128)(4,1)S(1)}, s32[16,1]{0,1:T(1,128)S(1)}) fusion(s32[64,8]{0,1:T(8,128)} %param.6, s32[]{:T(128)S(6)} %select_n.137, s32[]{:T(128)S(6)} %select_n.140), kind=kLoop, calls=%fused_computation.37 | loop fusion | flops 48 | bytes 152 | tf_op jit(solution)/shard_map/gt | solution.py:42
  0.8 0.1 copy.30
  1.0 0.1 add_reduce_fusion
  1.1 0.1 select_reduce_fusion
  1.2 0.0 copy-done
  1.2 0.6 gather_fusion
  1.8 0.5 broadcast_in_dim.72
  2.4 0.9 %constant_dynamic-update-slice_fusion.7 = (bf16[8,8,128,128]{3,2,1,0:T(8,128)(2,1)S(1)}, bf16[1,8,128,128]{3,2,1,0:T(8,128)(2,1)}) fusion(bf16[8,8,128,128]{3,2,1,0:T(8,128)(2,1)S(1)} %broadcast_in_dim.72, s32[]{:T(128)S(6)} %select_n.140, bf16[8,128,128]{2,1,0:T(8,128)(2,1)S(1)} %gather_fusion, pred[8]{0:T(512)(128)(4,1)S(1)} %compare_and_fusion.1), kind=kLoop, calls=%fused_computation.35 | loop fusion | flops 131072 | bytes 786948 | tf_op jit(solution)/shard_map/dynamic_update_slice | solution.py:59
  3.2 3.0 %collective-permute-start = (bf16[1,8,128,128]{3,2,1,0:T(8,128)(2,1)}, bf16[1,8,128,128]{3,2,1,0:T(8,128)(2,1)}, u32[]{:S(2)}, u32[]{:S(2)}) collective-permute-start(bf16[1,8,128,128]{3,2,1,0:T(8,128)(2,1)} %get-tuple-element.8), channel_id=1, source_target_pairs={{0,1},{1,2},{2,3},{3,16},{16,17},{17,18},{18,19},{19,0},{4,5},{5,6... | collective-permute-start | bytes 786440 | tf_op jit(solution)/shard_map/ppermute | solution.py:63
  6.3 3.0 %collective-permute-start.1 = (bf16[1,8,128,128]{3,2,1,0:T(8,128)(2,1)}, bf16[1,8,128,128]{3,2,1,0:T(8,128)(2,1)S(1)}, u32[]{:S(2)}, u32[]{:S(2)}) collective-permute-start(bf16[1,8,128,128]{3,2,1,0:T(8,128)(2,1)} %get-tuple-element.8), channel_id=1, source_target_pairs={{0,19},{1,0},{2,1},{3,2},{16,3},{17,16},{18,17},{19,18},{4,23},{5,... | collective-permute-start | bytes 786440 | tf_op jit(solution)/shard_map/ppermute | solution.py:68
  9.2 0.0 copy-done.3
  9.2 0.1 convert_compare_fusion
  9.3 0.1 copy.27
  9.4 0.1 copy.28
  9.5 0.8 %dynamic-slice_compare_fusion.1 = pred[16,2]{0,1:T(4,128)(4,1)S(1)} fusion(s32[64,8]{0,1:T(8,128)} %param.7, s32[]{:T(128)S(6)} %select_n.137, s32[]{:T(128)S(6)} %select_n.138), kind=kLoop, calls=%fused_computation.40 | loop fusion | flops 32 | bytes 168 | tf_op jit(solution)/shard_map/gt | solution.py:119
  10.3 0.1 broadcast_bitcast_fusion
  10.4 0.1 compare_and_fusion
  10.4 0.1 min.15
  10.5 0.1 add.203
  10.6 0.0 copy-done.2
  10.6 0.1 subtract_convert_fusion
  10.7 6.0 %collective-permute-done = bf16[1,8,128,128]{3,2,1,0:T(8,128)(2,1)} collective-permute-done((bf16[1,8,128,128]{3,2,1,0:T(8,128)(2,1)}, bf16[1,8,128,128]{3,2,1,0:T(8,128)(2,1)}, u32[]{:S(2)}, u32[]{:S(2)}) %collective-permute-start) | collective-permute-done | bytes 262176 | tf_op jit(solution)/shard_map/ppermute | solution.py:63
  16.7 0.0 collective-permute-start.2
  16.7 15.1 %all_gather.3 = bf16[1024,256]{1,0:T(8,128)(2,1)S(1)} all-gather(bf16[128,256]{1,0:T(8,128)(2,1)S(1)} %subtract_convert_fusion), channel_id=1, replica_groups=mesh['layer'=2,'row'=4,'col'=4] {'layer','row'}, dimensions={0}, use_global_device_ids=true | all-gather | bytes 589824 | tf_op jit(solution)/shard_map/all_gather | solution.py:79
  31.8 0.0 collective-permute-done.1
  31.8 0.3 collective-permute-start.3
  32.2 0.1 copy.29
  32.2 0.1 copy.26
  32.3 0.1 broadcast_in_dim.69
  32.5 1.4 %copy.34 = pred[2048,256]{1,0:T(32,128)(4,1)} copy(pred[2048,256]{0,1:T(32,128)(4,1)S(1)} %bitcast.45) | data formatting | bytes 1048576 | tf_op jit(solution)/shard_map/gt | solution.py:119
  33.9 0.0 collective-permute-done.2
  33.9 1.7 %collective-permute-start.4 = (bf16[1,8,128,128]{3,2,1,0:T(8,128)(2,1)}, bf16[1,8,128,128]{3,2,1,0:T(8,128)(2,1)S(1)}, u32[]{:S(2)}, u32[]{:S(2)}) collective-permute-start(bf16[1,8,128,128]{3,2,1,0:T(8,128)(2,1)} %collective-permute-done.2), channel_id=1, source_target_pairs={{0,1},{1,2},{2,3},{3,16},{16,17},{17,18},{18,19},{19,0},{4,5},{5,6... | collective-permute-start | bytes 786440 | tf_op jit(solution)/shard_map/ppermute | solution.py:63
  35.6 1.0 %constant_dynamic-update-slice_fusion.6 = bf16[8,8,128,128]{3,2,1,0:T(8,128)(2,1)S(1)} fusion(bf16[8,8,128,128]{3,2,1,0:T(8,128)(2,1)S(1)} %get-tuple-element.7, bf16[1,8,128,128]{3,2,1,0:T(8,128)(2,1)} %collective-permute-done, s32[]{:T(128)S(6)} %select_n.146), kind=kLoop, calls=%fused_computation.34 | loop fusion | bytes 524292 | tf_op jit(solution)/shard_map/dynamic_update_slice | solution.py:64
  36.7 9.8 %collective-permute-done.3 = bf16[1,8,128,128]{3,2,1,0:T(8,128)(2,1)} collective-permute-done((bf16[1,8,128,128]{3,2,1,0:T(8,128)(2,1)S(1)}, bf16[1,8,128,128]{3,2,1,0:T(8,128)(2,1)}, u32[]{:S(2)}, u32[]{:S(2)}) %collective-permute-start.3) | collective-permute-done | bytes 262176 | tf_op jit(solution)/shard_map/ppermute | solution.py:68
  46.5 0.0 collective-permute-start.5
  46.5 1.0 %constant_dynamic-update-slice_fusion.4 = bf16[8,8,128,128]{3,2,1,0:T(8,128)(2,1)S(1)} fusion(bf16[8,8,128,128]{3,2,1,0:T(8,128)(2,1)S(1)} %constant_dynamic-update-slice_fusion.5, bf16[1,8,128,128]{3,2,1,0:T(8,128)(2,1)} %collective-permute-done.2, s32[]{:T(128)S(6)} %select_n.150), kind=kLoop, calls=%fused_computation.32 | loop fusion | bytes 524292 | tf_op jit(solution)/shard_map/dynamic_update_slice | solution.py:64
  47.5 0.0 collective-permute-done.4
  47.5 2.1 %collective-permute-start.6 = (bf16[1,8,128,128]{3,2,1,0:T(8,128)(2,1)S(1)}, bf16[1,8,128,128]{3,2,1,0:T(8,128)(2,1)S(1)}, u32[]{:S(2)}, u32[]{:S(2)}) collective-permute-start(bf16[1,8,128,128]{3,2,1,0:T(8,128)(2,1)S(1)} %collective-permute-done.4), channel_id=1, source_target_pairs={{0,1},{1,2},{2,3},{3,16},{16,17},{17,18},{18,19},{19,0},{4,5},{5,6... | collective-permute-start | bytes 786440 | tf_op jit(solution)/shard_map/ppermute | solution.py:63
  49.6 1.0 %constant_dynamic-update-slice_fusion.3 = bf16[8,8,128,128]{3,2,1,0:T(8,128)(2,1)S(1)} fusion(bf16[8,8,128,128]{3,2,1,0:T(8,128)(2,1)S(1)} %constant_dynamic-update-slice_fusion.4, bf16[1,8,128,128]{3,2,1,0:T(8,128)(2,1)} %collective-permute-done.3, s32[]{:T(128)S(6)} %select_n.152), kind=kLoop, calls=%fused_computation.31 | loop fusion | bytes 524292 | tf_op jit(solution)/shard_map/dynamic_update_slice | solution.py:69
  50.6 8.1 %collective-permute-done.5 = bf16[1,8,128,128]{3,2,1,0:T(8,128)(2,1)S(1)} collective-permute-done((bf16[1,8,128,128]{3,2,1,0:T(8,128)(2,1)}, bf16[1,8,128,128]{3,2,1,0:T(8,128)(2,1)S(1)}, u32[]{:S(2)}, u32[]{:S(2)}) %collective-permute-start.5) | collective-permute-done | bytes 262176 | tf_op jit(solution)/shard_map/ppermute | solution.py:68
  58.7 0.0 collective-permute-done.6
  58.8 3.0 %gather_fusion.1 = bf16[128,128,128]{2,1,0:T(8,128)(2,1)} fusion(bf16[64,128,128]{2,1,0:T(8,128)(2,1)S(1)} %bitcast.42, s32[1024]{0:T(1024)S(1)} %pad_clamp_fusion), kind=kCustom, calls=%fused_computation.1 | custom fusion | bytes 8389120 | tf_op jit(solution)/shard_map/jit(_take)/gather | solution.py:93
  61.8 2.6 %select_bitcast_fusion = bf16[16,128,128,8]{2,1,3,0:T(8,128)(2,1)S(1)} fusion(bf16[16,8,128,128]{3,2,1,0:T(8,128)(2,1)} %bitcast.43, pred[16,8]{1,0:T(8,128)(4,1)S(1)} %copy.29, pred[16,8]{1,0:T(8,128)(4,1)S(1)} %copy.26), kind=kLoop, calls=%fused_computation.4 | loop fusion | flops 4194304 | bytes 8388864 | tf_op jit(solution)/shard_map/ijab,jbc->iac/dot_general | solution.py:97
  64.4 0.0 copy-start.1
  64.4 3.5 %copy.32 = bf16[16,128,128,8]{2,3,1,0:T(8,128)(2,1)S(1)} copy(bf16[16,128,128,8]{2,1,3,0:T(8,128)(2,1)S(1)} %select_bitcast_fusion) | data formatting | bytes 8388608 | tf_op jit(solution)/shard_map/ijab,jbc->iac/dot_general | solution.py:97
  68.0 0.0 copy-done.1
  68.0 2.3 %fusion.8 = bf16[2048,256]{1,0:T(8,128)(2,1)} fusion(pred[2048,256]{1,0:T(32,128)(4,1)S(1)} %copy-done.1, bf16[8,128,256]{2,1,0:T(8,128)(2,1)S(1)} %bitcast.46, bf16[2048,128,8]{1,2,0:T(8,128)(2,1)S(1)} %bitcast.44), kind=kOutput, calls=%fused_computation.7 | convolution fusion | flops 1074790400 | bytes 6291456 | tf_op jit(solution)/shard_map/ijab,jbc->iac/dot_general | solution.py:97
  (20 shorter events, 0.3 us)
Async XLA Ops:
  0.0 1.2 %copy-start = (bf16[2048,128]{1,0:T(8,128)(2,1)S(1)}, bf16[2048,128]{1,0:T(8,128)(2,1)}, u32[]{:S(2)}) copy-start(bf16[2048,128]{1,0:T(8,128)(2,1)} %param.4) | copy-start | bytes 1572868
  0.0 9.2 %copy-start.3 = (s32[64,8]{0,1:T(8,128)S(1)}, s32[64,8]{0,1:T(8,128)}, u32[]{:S(2)}) copy-start(s32[64,8]{0,1:T(8,128)} %param.6) | copy-start | bytes 6148
  0.0 10.6 %copy-start.2 = (bf16[128,256]{1,0:T(8,128)(2,1)S(1)}, bf16[128,256]{1,0:T(8,128)(2,1)}, u32[]{:S(2)}) copy-start(bf16[128,256]{1,0:T(8,128)(2,1)} %param.5) | copy-start | bytes 196612
  3.2 13.5 %collective-permute-start = (bf16[1,8,128,128]{3,2,1,0:T(8,128)(2,1)}, bf16[1,8,128,128]{3,2,1,0:T(8,128)(2,1)}, u32[]{:S(2)}, u32[]{:S(2)}) collective-permute-start(bf16[1,8,128,128]{3,2,1,0:T(8,128)(2,1)} %get-tuple-element.8), channel_id=1, source_target_pairs={{0,1},{1,2},{2,3},{3,16},{16,17},{17,18},{18,19},{19,0},{4,5},{5,6... | collective-permute-start | bytes 786440 | tf_op jit(solution)/shard_map/ppermute | solution.py:63
  6.3 25.5 %collective-permute-start.1 = (bf16[1,8,128,128]{3,2,1,0:T(8,128)(2,1)}, bf16[1,8,128,128]{3,2,1,0:T(8,128)(2,1)S(1)}, u32[]{:S(2)}, u32[]{:S(2)}) collective-permute-start(bf16[1,8,128,128]{3,2,1,0:T(8,128)(2,1)} %get-tuple-element.8), channel_id=1, source_target_pairs={{0,19},{1,0},{2,1},{3,2},{16,3},{17,16},{18,17},{19,18},{4,23},{5,... | collective-permute-start | bytes 786440 | tf_op jit(solution)/shard_map/ppermute | solution.py:68
  16.7 17.2 %collective-permute-start.2 = (bf16[1,8,128,128]{3,2,1,0:T(8,128)(2,1)}, bf16[1,8,128,128]{3,2,1,0:T(8,128)(2,1)}, u32[]{:S(2)}, u32[]{:S(2)}) collective-permute-start(bf16[1,8,128,128]{3,2,1,0:T(8,128)(2,1)} %collective-permute-done), channel_id=1, source_target_pairs={{0,1},{1,2},{2,3},{3,16},{16,17},{17,18},{18,19},{19,0},{4,5},{5,6... | collective-permute-start | bytes 786440 | tf_op jit(solution)/shard_map/ppermute | solution.py:63
  31.8 14.7 %collective-permute-start.3 = (bf16[1,8,128,128]{3,2,1,0:T(8,128)(2,1)S(1)}, bf16[1,8,128,128]{3,2,1,0:T(8,128)(2,1)}, u32[]{:S(2)}, u32[]{:S(2)}) collective-permute-start(bf16[1,8,128,128]{3,2,1,0:T(8,128)(2,1)S(1)} %collective-permute-done.1), channel_id=1, source_target_pairs={{0,19},{1,0},{2,1},{3,2},{16,3},{17,16},{18,17},{19,18},{4,23},{5,... | collective-permute-start | bytes 786440 | tf_op jit(solution)/shard_map/ppermute | solution.py:68
  33.9 13.6 %collective-permute-start.4 = (bf16[1,8,128,128]{3,2,1,0:T(8,128)(2,1)}, bf16[1,8,128,128]{3,2,1,0:T(8,128)(2,1)S(1)}, u32[]{:S(2)}, u32[]{:S(2)}) collective-permute-start(bf16[1,8,128,128]{3,2,1,0:T(8,128)(2,1)} %collective-permute-done.2), channel_id=1, source_target_pairs={{0,1},{1,2},{2,3},{3,16},{16,17},{17,18},{18,19},{19,0},{4,5},{5,6... | collective-permute-start | bytes 786440 | tf_op jit(solution)/shard_map/ppermute | solution.py:63
  46.5 12.2 %collective-permute-start.5 = (bf16[1,8,128,128]{3,2,1,0:T(8,128)(2,1)}, bf16[1,8,128,128]{3,2,1,0:T(8,128)(2,1)S(1)}, u32[]{:S(2)}, u32[]{:S(2)}) collective-permute-start(bf16[1,8,128,128]{3,2,1,0:T(8,128)(2,1)} %collective-permute-done.3), channel_id=1, source_target_pairs={{0,19},{1,0},{2,1},{3,2},{16,3},{17,16},{18,17},{19,18},{4,23},{5,... | collective-permute-start | bytes 786440 | tf_op jit(solution)/shard_map/ppermute | solution.py:68
  47.5 11.2 %collective-permute-start.6 = (bf16[1,8,128,128]{3,2,1,0:T(8,128)(2,1)S(1)}, bf16[1,8,128,128]{3,2,1,0:T(8,128)(2,1)S(1)}, u32[]{:S(2)}, u32[]{:S(2)}) collective-permute-start(bf16[1,8,128,128]{3,2,1,0:T(8,128)(2,1)S(1)} %collective-permute-done.4), channel_id=1, source_target_pairs={{0,1},{1,2},{2,3},{3,16},{16,17},{17,18},{18,19},{19,0},{4,5},{5,6... | collective-permute-start | bytes 786440 | tf_op jit(solution)/shard_map/ppermute | solution.py:63
  64.4 3.6 %copy-start.1 = (pred[2048,256]{1,0:T(32,128)(4,1)S(1)}, pred[2048,256]{1,0:T(32,128)(4,1)}, u32[]{:S(2)}) copy-start(pred[2048,256]{1,0:T(32,128)(4,1)} %copy.34) | copy-start | bytes 1572868
